TPU v7x, 32 devices: a whole 2x2x4 slice. The times are simulated.
32 devices in a mesh: bucket: 8 (over z, x), rel: 4 (over y, core).
Axes of the slice: x: 2, y: 2, z: 4, core: 2. Of those that a mesh axis runs over, the one named last changes fastest.
Arguments:
- left_rows: float32 [8192, 512], P(('bucket', 'rel')), may hold values from -1.2 to 1.2
- left_state: float32 [8192], P(('bucket', 'rel')), may hold values from 1e-06 to 0.0001
- right_rows: float32 [8192, 512], P(('bucket', 'rel')), may hold values from -1.2 to 1.2
- right_state: float32 [8192], P(('bucket', 'rel')), may hold values from 1e-06 to 0.0001
- relations: bfloat16 [4, 512, 512], P('rel'), may hold values from -0.25 to 0.25
- fetch_ids: int32 [8, 4, 4], P('bucket', 'rel'), may hold values from 0 to 3
- edge_left: int32 [8, 4, 2, 512], P('bucket', 'rel'), may hold values from 0 to 255
- edge_right: int32 [8, 4, 2, 512], P('bucket', 'rel'), may hold values from 0 to 255
- edge_slot: int32 [8, 4, 2, 512], P('bucket', 'rel'), may hold values from 0 to 1
- edge_weight: int32 [8, 4, 2, 512], P('bucket', 'rel'), may hold values from 1 to 4
- matching: int32 [1], replicated, may hold values from 1 to 7
Outputs:
- left_out: float32 [8192, 512], P(('bucket', 'rel'))
- left_state_out: float32 [8192], P(('bucket', 'rel'))
- right_out: float32 [8192, 512], P(('bucket', 'rel'))
- right_state_out: float32 [8192], P(('bucket', 'rel'))
- rel_grad: float32 [4, 512, 512], P('rel')
Inputs may be any that keep to these rules, and one draw needn't show every extreme that they name: Bucket b is paired with bucket b XOR matching.
All inputs are finite; a program needn't handle non-finite values.
Results may differ from a plain program's by a relative error of at most 0.0015.
The roundings to bfloat16 on the way count: a program that leaves them out, or rounds other values in their place, can miss the bound.
Values may be sent and summed in bfloat16 or wider, within the bound.
No kernel may reach another device: no remote copies, remote signals or barrier semaphores. Data moves between devices by JAX's collectives and lax.ppermute only.
A program may use at most 64 MiB of HBM per device.

v0:
```python
import jax
import jax.numpy as jnp
from jax import lax
from jax.sharding import PartitionSpec as P

learn_rate = 0.1


def edge_targets(edge_left, edge_right, edge_slot, edge_weight, block_len):
    table = jnp.zeros((2, block_len, block_len), jnp.float32)
    table = table.at[edge_slot, edge_left, edge_right].add(edge_weight.astype(jnp.float32))
    return [table[0], table[1]]


def adagrad(table, state, gradient):
    state_new = state + jnp.mean(gradient * gradient, axis=1)
    return (table - learn_rate * gradient / jnp.sqrt(state_new)[:, None], state_new)


def one_round(
    left_block,
    left_st,
    right_block,
    right_st,
    rel_pair,
    edge_left,
    edge_right,
    edge_slot,
    edge_weight,
):
    block_len = left_block.shape[0]
    left_half = left_block.astype(jnp.bfloat16)
    right_half = right_block.astype(jnp.bfloat16)
    targets = edge_targets(edge_left, edge_right, edge_slot, edge_weight, block_len)
    grad_left = jnp.zeros(left_block.shape, jnp.float32)
    grad_right = jnp.zeros(right_block.shape, jnp.float32)
    rel_grads = []
    for slot_index in range(2):
        matrix = rel_pair[slot_index]
        projected = jnp.dot(left_half, matrix, preferred_element_type=jnp.float32).astype(
            jnp.bfloat16
        )
        scores = jnp.dot(projected, right_half.T, preferred_element_type=jnp.float32)
        score_grad = ((jax.nn.sigmoid(scores) - targets[slot_index]) / block_len).astype(
            jnp.bfloat16
        )
        carried = jnp.dot(score_grad, right_half, preferred_element_type=jnp.float32).astype(
            jnp.bfloat16
        )
        grad_left = grad_left + jnp.dot(carried, matrix.T, preferred_element_type=jnp.float32)
        grad_right = grad_right + jnp.dot(
            score_grad.T, projected, preferred_element_type=jnp.float32
        )
        rel_grads.append(jnp.dot(left_half.T, carried, preferred_element_type=jnp.float32))
    left_new, left_st_new = adagrad(left_block, left_st, grad_left)
    right_new, right_st_new = adagrad(right_block, right_st, grad_right)
    return (left_new, left_st_new, right_new, right_st_new, rel_grads)


def partner_blocks(row_block, state_block, switch):
    block_len = row_block.shape[0]
    width = row_block.shape[1]
    partner = jnp.bitwise_xor(lax.axis_index("bucket"), switch)
    portion = (
        lax.all_gather(row_block, "bucket", axis=0, tiled=True),
        lax.all_gather(state_block, "bucket", axis=0, tiled=True),
    )
    block_count = portion[0].shape[0] // block_len
    owners = jnp.arange(block_count, dtype=jnp.int32)
    chosen = owners == partner
    rows_part = portion[0].reshape(block_count, block_len, width)
    states_part = portion[1].reshape(block_count, block_len)
    rows_new = jnp.sum(jnp.where(chosen[:, None, None], rows_part, jnp.float32(0.0)), axis=0)
    states_new = jnp.sum(jnp.where(chosen[:, None], states_part, jnp.float32(0.0)), axis=0)
    return (rows_new, states_new)


def reduce_gradients(gradients, rel_ids, rel_total, width):
    stacked = jnp.stack(gradients)
    own_rows = rel_total // lax.axis_size("rel") * width
    rel_count_piece = own_rows * lax.axis_size("rel") // width
    rel_list = jnp.arange(rel_count_piece, dtype=jnp.int32)
    weights = (rel_ids[:, None] == rel_list[None, :]).astype(jnp.float32)
    term = jnp.einsum("sk,sde->kde", weights, stacked, precision=lax.Precision.HIGHEST)
    partial_sum = lax.psum_scatter(
        term.reshape(rel_count_piece * width, width), "rel", scatter_dimension=0, tiled=True
    )
    return lax.psum(partial_sum, "bucket")


def on_device(
    left_rows,
    left_state,
    right_rows,
    right_state,
    relations,
    fetch_ids,
    edge_left,
    edge_right,
    edge_slot,
    edge_weight,
    matching,
):
    width = relations.shape[1]
    rel_table = lax.all_gather(relations, "rel", axis=0, tiled=True)
    rel_total = rel_table.shape[0]
    rel_ids = fetch_ids[0, 0]
    switch = matching[0]
    table_left, state_left = (left_rows, left_state)
    row_block, state_block = (right_rows, right_state)
    gradients = []
    for round_index in range(2):
        rel_pair = jnp.take(rel_table, rel_ids[2 * round_index : 2 * round_index + 2], axis=0)
        table_left, state_left, row_block, state_block, rel_grads = one_round(
            table_left,
            state_left,
            row_block,
            state_block,
            rel_pair,
            edge_left[0, 0, round_index],
            edge_right[0, 0, round_index],
            edge_slot[0, 0, round_index],
            edge_weight[0, 0, round_index],
        )
        gradients.extend(rel_grads)
        if round_index == 0:
            row_block, state_block = partner_blocks(row_block, state_block, switch)
    owned = reduce_gradients(gradients, rel_ids, rel_total, width)
    return (table_left, state_left, row_block, state_block, owned.reshape(-1, width, width))


def solution(mesh):
    in_specs = (
        P(("bucket", "rel"), None),
        P(("bucket", "rel")),
        P(("bucket", "rel"), None),
        P(("bucket", "rel")),
        P("rel", None, None),
        P("bucket", "rel", None),
        P("bucket", "rel", None, None),
        P("bucket", "rel", None, None),
        P("bucket", "rel", None, None),
        P("bucket", "rel", None, None),
        P(),
    )
    out_specs = (
        P(("bucket", "rel"), None),
        P(("bucket", "rel")),
        P(("bucket", "rel"), None),
        P(("bucket", "rel")),
        P("rel", None, None),
    )
    return jax.shard_map(
        on_device, mesh=mesh, in_specs=in_specs, out_specs=out_specs, check_vma=False
    )
```

profile of v0, /device:TPU:0, one launch (start us, length us, event | category | flops | bytes accessed | tf_op | source)
XLA Modules:
  0.0 281.4 jit_solution(3566939604815437510)
XLA Ops:
  7.2 0.7 all-gather.4.cloned.1.call-update
  8.0 1.1 convert_element_type.65
  9.0 1.1 convert_element_type.63
  10.1 0.8 slice_convert_fusion
  10.9 0.8 or_select_fusion
  11.7 31.3 %scatter_fusion = f32[2,256,256]{2,1,0:T(8,128)S(1)} fusion(f32[2,256,256]{2,1,0:T(8,128)S(1)} %broadcast.145.clone, s32[512]{0:T(512)S(1)} %bitcast.126, f32[512]{0:T(512)S(1)} %bitcast.131), kind=kCustom, calls=%fused_computation.2 | custom fusion | flops 512 | bytes 12288 | tf_op jit(solution)/shard_map/scatter-add | solution.py:11
  43.0 0.6 compare_and_fusion
  43.6 2.2 gather_fusion
  46.0 0.3 convolution_convert_fusion.5
  46.4 0.3 convolution_convert_fusion.7
  46.8 0.3 fusion.22
  47.0 0.3 fusion.23
  47.6 0.4 multiply_reduce_fusion.2
  48.0 0.6 fusion.39
  48.6 0.9 divide_subtract_fusion.2
  50.4 31.3 %scatter_fusion.1 = f32[2,256,256]{2,1,0:T(8,128)S(1)} fusion(f32[2,256,256]{2,1,0:T(8,128)S(1)} %broadcast.145.clone.1, s32[512]{0:T(512)S(1)} %bitcast.125, f32[512]{0:T(512)S(1)} %bitcast.130), kind=kCustom, calls=%fused_computation.3 | custom fusion | flops 512 | bytes 12288 | tf_op jit(solution)/shard_map/scatter-add | solution.py:11
  81.8 0.5 iota_compare_fusion.1
  82.3 3.2 %gather_fusion.1 = bf16[2,512,512]{2,1,0:T(8,128)(2,1)} fusion(bf16[4,512,512]{2,1,0:T(8,128)(2,1)} %all-gather.4.cloned.1.call-done, s32[1024]{0:T(1024)S(1)} %get-tuple-element.30), kind=kCustom, calls=%fused_computation.1.clone | custom fusion | bytes 2097160 | tf_op jit(solution)/shard_map/jit(_take)/gather | solution.py:113
  85.7 1.3 convolution_bitcast_fusion.2
  87.2 1.3 convolution_bitcast_fusion.3
  88.6 0.3 fusion.24
  88.9 0.4 multiply_reduce_fusion.3
  89.7 0.3 convolution_convert_fusion.1
  90.0 1.0 convolution_convert_fusion.3
  91.0 34.2 %all-gather.6.cloned.1.call-done = f32[2048,512]{1,0:T(8,128)} async-done(((f32[256,512]{1,0:T(8,128)}), f32[2048,512]{1,0:T(8,128)}) %all-gather.6.cloned.1.call-update) | async-done | bytes 4194320 | tf_op jit(solution)/shard_map/all_gather | solution.py:65
  125.2 2.9 %select_reduce_fusion = f32[256,512]{1,0:T(8,128)S(1)} fusion(f32[8,256,512]{2,1,0:T(8,128)} %bitcast.128, pred[8]{0:T(512)(128)(4,1)S(1)} %copy-done.14), kind=kLoop, calls=%fused_computation.5 | loop fusion | flops 1966080 | bytes 4718600 | tf_op jit(solution)/shard_map/reduce_sum | solution.py:73
  128.2 0.3 fusion.20
  128.7 0.3 fusion.21
  129.2 0.4 copy-done.7
  129.6 0.3 convolution_bitcast_fusion
  130.0 0.3 convolution_bitcast_fusion.1
  130.4 2.4 pad_maximum_fusion
  132.8 5.5 %copy.25 = f32[4,512,512]{2,0,1:T(4,128)} copy(f32[4,512,512]{1,2,0:T(8,128)} %pad_maximum_fusion) | data formatting | bytes 8388608 | tf_op jit(solution)/shard_map/stack | solution.py:79
  138.2 6.2 %fusion.32 = f32[4,512,512]{2,0,1:T(4,128)S(1)} fusion(f32[4,512,512]{2,0,1:T(4,128)} %copy.25, s32[4]{0:T(128)S(1)} %bitcast.132), kind=kOutput, calls=%fused_computation.98 | convolution fusion | flops 50331664 | bytes 8388624 | tf_op jit(solution)/shard_map/sk,sde->kde/dot_general | solution.py:84
  144.4 3.2 %copy.26 = f32[4,512,512]{2,1,0:T(8,128)} copy(f32[4,512,512]{2,0,1:T(4,128)S(1)} %fusion.32) | data formatting | bytes 8388608 | tf_op jit(solution)/shard_map/sk,sde->kde/dot_general | solution.py:84
  147.7 0.6 copy-done.13
  148.3 18.1 %all-gather = f32[8,1,256]{2,1,0:T(1,128)S(1)} all-gather(f32[1,1,256]{2,1,0:T(1,128)S(1)} %bitcast.133), channel_id=1, replica_groups=mesh['bucket'=8,'rel'=4] {'bucket'}, dimensions={0}, use_global_device_ids=true | all-gather | bytes 9216 | tf_op jit(solution)/shard_map/all_gather | solution.py:66
  166.6 1.2 fusion.41
  167.8 1.1 fusion.25
  168.9 2.0 multiply_reduce_fusion
  170.9 20.1 %reduce-scatter.2.cloned.1.call-done = f32[512,512]{1,0:T(8,128)} async-done(((f32[2048,512]{1,0:T(8,128)}), f32[512,512]{1,0:T(8,128)}) %reduce-scatter.2.cloned.1.call-update) | async-done | bytes 1048592 | tf_op jit(solution)/shard_map/reduce_scatter | solution.py:85
  191.0 0.6 fusion.37
  191.6 1.5 multiply_reduce_fusion.1
  193.0 0.6 fusion.38
  193.6 2.0 divide_subtract_fusion
  195.6 1.0 divide_subtract_fusion.1
  196.6 76.0 %all-reduce.2.cloned.1.call-done = f32[1,512,512]{2,1,0:T(8,128)} async-done(((f32[1,512,512]{2,1,0:T(8,128)}), f32[1,512,512]{2,1,0:T(8,128)}) %all-reduce.2.cloned.1.call-update) | async-done | bytes 1048592 | tf_op jit(solution)/shard_map/psum | solution.py:88
  272.6 2.3 copy.35
  (56 shorter events, 2.3 us)
Async XLA Ops:
  7.2 35.9 %copy-start.11 = (s32[1,1,4]{2,1,0:T(1,128)S(1)}, s32[1,1,4]{2,1,0:T(1,128)}, u32[]{:S(2)}) copy-start(s32[1,1,4]{2,1,0:T(1,128)} %param.18) | copy-start | bytes 52
  7.2 36.5 %all-gather.4.cloned.1.call-start = ((), (), s32[]{:S(2)}) async-start(), calls=%async_computation.1 | async-start | bytes 2621440 | tf_op jit(solution)/shard_map/all_gather | solution.py:105
  7.9 117.3 %all-gather.6.cloned.1.call-start = ((), (), s32[]{:S(2)}) async-start(), calls=%async_computation.2 | async-start | bytes 4718592 | tf_op jit(solution)/shard_map/all_gather | solution.py:65
  46.0 2.0 copy-start.17
  46.0 2.5 copy-start.6
  49.5 141.5 %reduce-scatter.2.cloned.1.call-start = ((), (), s32[]{:S(2)}) async-start(), calls=%async_computation.3 | async-start | bytes 5242880 | tf_op jit(solution)/shard_map/reduce_scatter | solution.py:85
  85.5 3.9 %copy-start.12 = (f32[256]{0:T(256)S(1)}, f32[256]{0:T(256)}, u32[]{:S(2)}) copy-start(f32[256]{0:T(256)} %param.14) | copy-start | bytes 3076
  85.5 3.9 %copy-start = (f32[256,512]{1,0:T(8,128)S(1)}, f32[256,512]{1,0:T(8,128)}, u32[]{:S(2)}) copy-start(f32[256,512]{1,0:T(8,128)} %param.13) | copy-start | bytes 1572868
  85.7 3.8 %copy-start.1 = (bf16[2,512,512]{2,1,0:T(8,128)(2,1)S(1)}, bf16[2,512,512]{2,1,0:T(8,128)(2,1)}, u32[]{:S(2)}) copy-start(bf16[2,512,512]{2,1,0:T(8,128)(2,1)} %gather_fusion.1) | copy-start | bytes 3145732
  85.7 3.8 %copy-start.16 = (pred[2]{0:T(512)(128)(4,1)S(1)}, pred[2]{0:T(512)(128)(4,1)}, u32[]{:S(2)}) copy-start(pred[2]{0:T(512)(128)(4,1)} %get-tuple-element.12) | copy-start | bytes 10
  88.6 36.6 %copy-start.14 = (pred[8]{0:T(512)(128)(4,1)S(1)}, pred[8]{0:T(512)(128)(4,1)}, u32[]{:S(2)}) copy-start(pred[8]{0:T(512)(128)(4,1)} %iota_compare_fusion.1) | copy-start | bytes 28
  89.5 35.7 %copy-start.4 = (bf16[256,512]{1,0:T(8,128)(2,1)}, bf16[256,512]{1,0:T(8,128)(2,1)S(1)}, u32[]{:S(2)}) copy-start(bf16[256,512]{1,0:T(8,128)(2,1)S(1)} %fusion.36) | copy-start | bytes 786436
  90.0 38.2 %copy-start.9 = (bf16[256,512]{1,0:T(8,128)(2,1)}, bf16[256,512]{1,0:T(8,128)(2,1)S(1)}, u32[]{:S(2)}) copy-start(bf16[256,512]{1,0:T(8,128)(2,1)S(1)} %convolution_convert_fusion.1) | copy-start | bytes 786436
  125.2 3.5 %copy-start.10 = (bf16[256,512]{1,0:T(8,128)(2,1)S(1)}, bf16[256,512]{1,0:T(8,128)(2,1)}, u32[]{:S(2)}) copy-start(bf16[256,512]{1,0:T(8,128)(2,1)} %convolution_convert_fusion.3) | copy-start | bytes 786436
  125.2 4.4 %copy-start.5 = (bf16[256,512]{1,0:T(8,128)(2,1)S(1)}, bf16[256,512]{1,0:T(8,128)(2,1)}, u32[]{:S(2)}) copy-start(bf16[256,512]{1,0:T(8,128)(2,1)} %copy-done.4) | copy-start | bytes 786436
  128.1 2.2 copy-start.2
  128.1 2.2 copy-start.3
  129.0 0.7 copy-start.7
  147.7 0.7 copy-start.13
  147.7 18.8 %copy-start.15 = (pred[8]{0:T(512)(128)(4,1)S(1)}, pred[8]{0:T(512)(128)(4,1)}, u32[]{:S(2)}) copy-start(pred[8]{0:T(512)(128)(4,1)} %iota_compare_fusion.1) | copy-start | bytes 28
  147.7 18.9 %copy-start.8 = (bf16[256,256]{1,0:T(8,128)(2,1)S(1)}, bf16[256,256]{1,0:T(8,128)(2,1)}, u32[]{:S(2)}) copy-start(bf16[256,256]{1,0:T(8,128)(2,1)} %copy-done.7) | copy-start | bytes 393220
  147.7 124.9 %all-reduce.2.cloned.1.call-start = ((), (), s32[]{:S(2)}) async-start(), calls=%async_computation.4 | async-start | bytes 2097152 | tf_op jit(solution)/shard_map/psum | solution.py:88
Sparse Core Ops, SparseCore 0:
  9.5 25.2 all-gather.3
  49.6 75.5 all-gather.5
  147.8 43.1 reduce-scatter.1
  194.4 78.2 all-reduce.1
where the time goes:
time: 282 us; the launch traced here: 281 us
  waiting for transfers between devices  131 us (46%)
  other arithmetic  78.9 us (28%)
  matrix products  20.7 us (7%)
  blocking collectives  18.1 us (6%)
  local copies, waits for them, and re-layouts  17.5 us (6%)
  between operations  14.8 us (5%)
    psum x1, waiting for transfers between devices, reduce_gradients(): return lax.psum(partial_sum, 'bucket')  76 us
    scatter-add x2, other arithmetic, edge_targets(): table.at[edge_slot, edge_left, edge_right]  62.6 us
    all_gather x1, waiting for transfers between devices, partner_blocks(): lax.all_gather(row_block, 'bucket', axis=0, tiled=True)  34.2 us
    reduce_scatter x1, waiting for transfers between devices, reduce_gradients(): lax.psum_scatter(term.reshape(rel_count_piece * width, width), 'rel', sca...  20.1 us
    all_gather x1, blocking collectives, partner_blocks(): lax.all_gather(state_block, 'bucket', axis=0, tiled=True)  18.1 us
    dot_general x1, matrix products, reduce_gradients(): jnp.einsum('sk,sde->kde', weights, stacked, precision=lax.Precision.HIGHEST)  6.2 us
  transfers between devices with their start and end apart: 4, of which 3 were waited for; matrix products, arithmetic and copies ran while one was open for 31% of the time, Pallas kernels for 0%

commit v1 on v0

--- a/solution.py
+++ b/solution.py
@@ -7,9 +7,20 @@
 
 
 def edge_targets(edge_left, edge_right, edge_slot, edge_weight, block_len):
-    table = jnp.zeros((2, block_len, block_len), jnp.float32)
-    table = table.at[edge_slot, edge_left, edge_right].add(edge_weight.astype(jnp.float32))
-    return [table[0], table[1]]
+    rows = jnp.arange(block_len, dtype=jnp.int32)
+    weight = edge_weight.astype(jnp.float32)
+    right_hot = (edge_right[:, None] == rows[None, :]).astype(jnp.bfloat16)
+    left_hot = edge_left[:, None] == rows[None, :]
+    targets = []
+    for slot_index in range(2):
+        scale = jnp.where(edge_slot == slot_index, weight, jnp.float32(0.0))
+        left_w = jnp.where(left_hot, scale[:, None], jnp.float32(0.0)).astype(jnp.bfloat16)
+        targets.append(
+            lax.dot_general(
+                left_w, right_hot, (((0,), (0,)), ((), ())), preferred_element_type=jnp.float32
+            )
+        )
+    return targets
 
 
 def adagrad(table, state, gradient):
@@ -58,21 +69,18 @@
 
 
 def partner_blocks(row_block, state_block, switch):
-    block_len = row_block.shape[0]
-    width = row_block.shape[1]
-    partner = jnp.bitwise_xor(lax.axis_index("bucket"), switch)
-    portion = (
-        lax.all_gather(row_block, "bucket", axis=0, tiled=True),
-        lax.all_gather(state_block, "bucket", axis=0, tiled=True),
-    )
-    block_count = portion[0].shape[0] // block_len
-    owners = jnp.arange(block_count, dtype=jnp.int32)
-    chosen = owners == partner
-    rows_part = portion[0].reshape(block_count, block_len, width)
-    states_part = portion[1].reshape(block_count, block_len)
-    rows_new = jnp.sum(jnp.where(chosen[:, None, None], rows_part, jnp.float32(0.0)), axis=0)
-    states_new = jnp.sum(jnp.where(chosen[:, None], states_part, jnp.float32(0.0)), axis=0)
-    return (rows_new, states_new)
+    count = lax.axis_size("bucket")
+
+    def exchange(offset):
+        pairs = [(b, b ^ offset) for b in range(count)]
+
+        def run(rows, states):
+            return (lax.ppermute(rows, "bucket", pairs), lax.ppermute(states, "bucket", pairs))
+
+        return run
+
+    branches = [exchange(offset) for offset in range(1, count)]
+    return lax.switch(switch - 1, branches, row_block, state_block)
 
 
 def reduce_gradients(gradients, rel_ids, rel_total, width):

time: 282 us -> 234 us (0.83)
  other arithmetic: 78.9 us -> 13.1 us
  waiting for transfers between devices: 131 us -> 161 us
  blocking collectives: 18.1 us -> 0 us
  starting transfers between devices: 0.34 us -> 4.01 us
    scatter-add x2 -> x0, other arithmetic: 62.6 us -> none  [edge_targets(): table.at[edge_slot, edge_left, edge_right]]
    all_gather x1 -> x0, waiting for transfers between devices: 34.2 us -> none  [partner_blocks(): lax.all_gather(row_block, 'bucket', axis=0, tiled=True)]
    ppermute x0 -> x2, waiting for transfers between devices: none -> 23.5 us  [the longest x1 23.4 us: run(): lax.ppermute(rows, 'bucket', pairs)]
    reduce_scatter x1, waiting for transfers between devices: 20.1 us -> 41.1 us  [reduce_gradients(): lax.psum_scatter(term.reshape(rel_count_piece * width, width), 'rel', sca...]
    all_gather x1, waiting for transfers between devices: 0.01 us -> 19.7 us  [on_device(): rel_table = lax.all_gather(relations, 'rel', axis=0, tiled=True)]
    all_gather x1 -> x0, blocking collectives: 18.1 us -> none  [partner_blocks(): lax.all_gather(state_block, 'bucket', axis=0, tiled=True)]
    ppermute x0 -> x2, starting transfers between devices: none -> 3.89 us  [the longest x1 3.39 us: run(): lax.ppermute(rows, 'bucket', pairs)]
    reduce_sum x2 -> x1, other arithmetic: 2.96 us -> 0.12 us  [adagrad(): state_new = state + jnp.mean(gradient * gradient, axis=1)]
  transfers between devices with their start and end apart: 4 -> 5, of which waited for: 3 -> 5; matrix products, arithmetic and copies ran while one was open for 31% -> 6% of each run, Pallas kernels for 0% -> 0%
where the time goes in v1:
time: 234 us
  waiting for transfers between devices  161 us (69%)
  matrix products  21.4 us (9%)
  local copies, waits for them, and re-layouts  19.1 us (8%)
  between operations  14.8 us (6%)
  other arithmetic  13.1 us (6%)
  starting transfers between devices  4.01 us (2%)
    psum x1, waiting for transfers between devices, reduce_gradients(): return lax.psum(partial_sum, 'bucket')  76.5 us
    reduce_scatter x1, waiting for transfers between devices, reduce_gradients(): lax.psum_scatter(term.reshape(rel_count_piece * width, width), 'rel', sca...  41.1 us
    ppermute x1, waiting for transfers between devices, run(): lax.ppermute(rows, 'bucket', pairs)  23.4 us
    all_gather x1, waiting for transfers between devices, on_device(): rel_table = lax.all_gather(relations, 'rel', axis=0, tiled=True)  19.7 us
    dot_general x1, matrix products, reduce_gradients(): jnp.einsum('sk,sde->kde', weights, stacked, precision=lax.Precision.HIGHEST)  6.2 us
    another operation x1, local copies, waits for them, and re-layouts, reduce_gradients(): stacked = jnp.stack(gradients)  5.55 us
  transfers between devices with their start and end apart: 5, of which 5 were waited for; matrix products, arithmetic and copies ran while one was open for 6% of the time, Pallas kernels for 0%

profile of v1, /device:TPU:0, one launch (start us, length us, event | category | flops | bytes accessed | tf_op | source)
XLA Modules:
  0.0 234.0 jit_solution(282676214583551554)
XLA Ops:
  7.2 0.7 all-gather.2.cloned.1.call-update
  8.6 1.1 convert_element_type.105
  9.7 1.8 convert_element_type.103
  11.4 0.8 compare_and_fusion
  12.3 0.8 fusion.57
  13.0 0.8 fusion.58
  13.8 1.4 compare_select_fusion
  15.2 19.7 %all-gather.2.cloned.1.call-done = bf16[4,512,512]{2,1,0:T(8,128)(2,1)} async-done(((bf16[1,512,512]{2,1,0:T(8,128)(2,1)}), bf16[4,512,512]{2,1,0:T(8,128)(2,1)}) %all-gather.2.cloned.1.call-update) | async-done | bytes 2097168 | tf_op jit(solution)/shard_map/all_gather | solution.py:113
  34.9 2.2 gather_fusion
  37.1 2.2 gather_fusion.1
  39.5 1.3 convolution_convert_fusion.5
  40.9 0.3 convolution_convert_fusion.7
  41.2 0.3 fusion.15
  41.5 0.5 fusion.16
  42.5 0.3 fusion.11
  42.8 0.5 fusion.17
  43.6 0.3 fusion.20
  43.9 0.4 multiply_reduce_fusion.9
  44.5 0.3 convolution_convert_fusion.1
  44.9 1.0 convolution_convert_fusion.3
  45.9 0.3 convolution_bitcast_fusion.2
  46.2 1.3 convolution_bitcast_fusion.3
  47.8 28.8 %conditional.4 = (f32[256,512]{1,0:T(8,128)}, f32[256]{0:T(256)}, f32[256,512]{1,0:T(8,128)S(1)}) conditional(s32[]{:T(128)} %bitcast.9, (f32[256,512]{1,0:T(8,128)S(1)}, f32[256,512]{1,0:T(8,128)S(1)}, f32[256]{0:T(256)S(1)}, f32[256,512]{1,0:T(8,128)S(1)}, f32[256,512]{1,0:T(8,128)S(1)}, ...), branch_computations={%region_2.4_spmd, %region_3.5_spmd, %region_4.6_spmd, %region_5.7_... | conditional | flops 655616 | bytes 5778540
  48.2 3.4 %collective-permute-start.8 = (f32[256,512]{1,0:T(8,128)S(1)}, f32[256,512]{1,0:T(8,128)}, u32[]{:S(2)}, u32[]{:S(2)}) collective-permute-start(f32[256,512]{1,0:T(8,128)S(1)} %divide_subtract_fusion.4), channel_id=1, source_target_pairs={{0,20},{4,16},{8,28},{12,24},{16,4},{20,0},{24,12},{28,8},{1,21},{... | collective-permute-start | bytes 1572872 | tf_op jit(solution)/shard_map/cond/branch_4_fun/ppermute | solution.py:78
  51.6 0.5 collective-permute-start.9
  52.1 23.4 %collective-permute-done.8 = f32[256,512]{1,0:T(8,128)} collective-permute-done((f32[256,512]{1,0:T(8,128)S(1)}, f32[256,512]{1,0:T(8,128)}, u32[]{:S(2)}, u32[]{:S(2)}) %collective-permute-start.8) | collective-permute-done | bytes 524320 | tf_op jit(solution)/shard_map/cond/branch_4_fun/ppermute | solution.py:78
  75.6 1.0 copy.70
  76.7 1.3 fusion.7
  78.0 0.5 fusion.18
  78.7 0.3 fusion.3
  79.0 1.2 fusion.19
  80.4 0.4 convolution_bitcast_fusion
  80.8 0.3 convolution_bitcast_fusion.1
  81.2 2.4 %pad_maximum_fusion = f32[4,512,512]{1,2,0:T(8,128)} fusion(f32[1,512,512]{1,2,0:T(8,128)S(1)} %convolution_bitcast_fusion, f32[1,512,512]{1,2,0:T(8,128)S(1)} %convolution_bitcast_fusion.1, f32[1,512,512]{1,2,0:T(8,128)S(1)} %convolution_bitcast_fusion.2, f32[1,512,512]{1,2,0:T(8,128)S(1)} %copy-done.2), kind=kLoop, calls=%fused_computation.23 | loop fusion | flops 3145728 | bytes 8388608 | tf_op jit(solution)/shard_map/stack | solution.py:87
  83.6 5.6 %copy.32 = f32[4,512,512]{2,0,1:T(4,128)} copy(f32[4,512,512]{1,2,0:T(8,128)} %pad_maximum_fusion) | data formatting | bytes 8388608 | tf_op jit(solution)/shard_map/stack | solution.py:87
  89.1 6.2 %fusion.39 = f32[4,512,512]{2,0,1:T(4,128)S(1)} fusion(f32[4,512,512]{2,0,1:T(4,128)} %copy.32, s32[4]{0:T(128)S(1)} %bitcast.96), kind=kOutput, calls=%fused_computation.116 | convolution fusion | flops 50331664 | bytes 8388624 | tf_op jit(solution)/shard_map/sk,sde->kde/dot_general | solution.py:92
  95.3 3.2 %copy.33 = f32[4,512,512]{2,1,0:T(8,128)} copy(f32[4,512,512]{2,0,1:T(4,128)S(1)} %fusion.39) | data formatting | bytes 8388608 | tf_op jit(solution)/shard_map/sk,sde->kde/dot_general | solution.py:92
  98.7 0.8 copy-done.9
  99.9 0.3 fusion.21
  100.2 2.0 multiply_reduce_fusion.7
  102.2 41.1 %reduce-scatter.2.cloned.1.call-done = f32[512,512]{1,0:T(8,128)} async-done(((f32[2048,512]{1,0:T(8,128)}), f32[512,512]{1,0:T(8,128)}) %reduce-scatter.2.cloned.1.call-update) | async-done | bytes 1048592 | tf_op jit(solution)/shard_map/reduce_scatter | solution.py:93
  143.3 1.2 fusion.55
  144.5 0.4 multiply_reduce_fusion.8
  144.9 0.6 fusion.56
  145.5 2.1 divide_subtract_fusion.7
  147.6 1.0 divide_subtract_fusion.8
  148.7 76.5 %all-reduce.2.cloned.1.call-done = f32[1,512,512]{2,1,0:T(8,128)} async-done(((f32[1,512,512]{2,1,0:T(8,128)}), f32[1,512,512]{2,1,0:T(8,128)}) %all-reduce.2.cloned.1.call-update) | async-done | bytes 1048592 | tf_op jit(solution)/shard_map/psum | solution.py:96
  225.2 2.3 copy.73
  (57 shorter events, 2.8 us)
Async XLA Ops:
  7.2 27.7 %all-gather.2.cloned.1.call-start = ((), (), s32[]{:S(2)}) async-start(), calls=%async_computation.1 | async-start | bytes 2621440 | tf_op jit(solution)/shard_map/all_gather | solution.py:113
  7.9 135.4 %reduce-scatter.2.cloned.1.call-start = ((), (), s32[]{:S(2)}) async-start(), calls=%async_computation.2 | async-start | bytes 5242880 | tf_op jit(solution)/shard_map/reduce_scatter | solution.py:93
  13.8 64.1 %copy-start.15 = (s32[1,1,1,512]{3,2,1,0:T(1,128)}, s32[1,1,1,512]{3,2,1,0:T(1,128)S(1)}, u32[]{:S(2)}) copy-start(s32[1,1,1,512]{3,2,1,0:T(1,128)S(1)} %get-tuple-element.244) | copy-start | bytes 6148
  39.3 1.6 copy-start.5
  42.0 2.3 copy-start.14
  42.0 2.3 copy-start.1
  44.4 3.5 %copy-start = (f32[256,512]{1,0:T(8,128)S(1)}, f32[256,512]{1,0:T(8,128)}, u32[]{:S(2)}) copy-start(f32[256,512]{1,0:T(8,128)} %param.22) | copy-start | bytes 1572868
  44.4 3.5 %copy-start.12 = (f32[256]{0:T(256)S(1)}, f32[256]{0:T(256)}, u32[]{:S(2)}) copy-start(f32[256]{0:T(256)} %param.23) | copy-start | bytes 3076
  44.5 3.2 %copy-start.6 = (bf16[256,512]{1,0:T(8,128)(2,1)}, bf16[256,512]{1,0:T(8,128)(2,1)S(1)}, u32[]{:S(2)}) copy-start(bf16[256,512]{1,0:T(8,128)(2,1)S(1)} %fusion.47) | copy-start | bytes 786436
  44.8 33.9 %copy-start.10 = (bf16[256,512]{1,0:T(8,128)(2,1)}, bf16[256,512]{1,0:T(8,128)(2,1)S(1)}, u32[]{:S(2)}) copy-start(bf16[256,512]{1,0:T(8,128)(2,1)S(1)} %convolution_convert_fusion.1) | copy-start | bytes 786436
  48.2 27.3 %collective-permute-start.8 = (f32[256,512]{1,0:T(8,128)S(1)}, f32[256,512]{1,0:T(8,128)}, u32[]{:S(2)}, u32[]{:S(2)}) collective-permute-start(f32[256,512]{1,0:T(8,128)S(1)} %divide_subtract_fusion.4), channel_id=1, source_target_pairs={{0,20},{4,16},{8,28},{12,24},{16,4},{20,0},{24,12},{28,8},{1,21},{... | collective-permute-start | bytes 1572872 | tf_op jit(solution)/shard_map/cond/branch_4_fun/ppermute | solution.py:78
  51.6 24.0 %collective-permute-start.9 = (f32[256]{0:T(256)S(1)}, f32[256]{0:T(256)}, u32[]{:S(2)}, u32[]{:S(2)}) collective-permute-start(f32[256]{0:T(256)S(1)} %get-tuple-element.225), channel_id=1, source_target_pairs={{0,20},{4,16},{8,28},{12,24},{16,4},{20,0},{24,12},{28,8},{1,21},{... | collective-permute-start | bytes 3080 | tf_op jit(solution)/shard_map/cond/branch_4_fun/ppermute | solution.py:78
  76.6 2.4 %copy-start.16 = (f32[1,1,1,512]{3,2,1,0:T(1,128)S(1)}, f32[1,1,1,512]{3,2,1,0:T(1,128)}, u32[]{:S(2)}) copy-start(f32[1,1,1,512]{3,2,1,0:T(1,128)} %get-tuple-element.238) | copy-start | bytes 6148
  76.6 3.8 %copy-start.7 = (bf16[256,512]{1,0:T(8,128)(2,1)S(1)}, bf16[256,512]{1,0:T(8,128)(2,1)}, u32[]{:S(2)}) copy-start(bf16[256,512]{1,0:T(8,128)(2,1)} %copy-done.6) | copy-start | bytes 786436
  77.9 3.2 %copy-start.2 = (f32[1,512,512]{1,2,0:T(8,128)S(1)}, f32[1,512,512]{1,2,0:T(8,128)}, u32[]{:S(2)}) copy-start(f32[1,512,512]{1,2,0:T(8,128)} %convolution_bitcast_fusion.3) | copy-start | bytes 3145732
  78.5 2.0 copy-start.8
  78.7 2.1 copy-start.3
  83.6 5.6 %copy-start.13 = (s32[1,1,4]{2,1,0:T(1,128)S(1)}, s32[1,1,4]{2,1,0:T(1,128)}, u32[]{:S(2)}) copy-start(s32[1,1,4]{2,1,0:T(1,128)} %param.25) | copy-start | bytes 52
  98.6 0.9 copy-start.9
  98.6 1.0 copy-start.11
  98.6 1.3 copy-start.4
  98.6 126.6 %all-reduce.2.cloned.1.call-start = ((), (), s32[]{:S(2)}) async-start(), calls=%async_computation.3 | async-start | bytes 2097152 | tf_op jit(solution)/shard_map/psum | solution.py:96
Sparse Core Ops, SparseCore 0:
  9.5 25.2 all-gather.1
  98.7 44.5 reduce-scatter.1
  146.8 78.3 all-reduce.1

commit v2 on v1

--- a/solution.py
+++ b/solution.py
@@ -83,17 +83,65 @@
     return lax.switch(switch - 1, branches, row_block, state_block)
 
 
+def axis_bits(axis):
+    count = lax.axis_size(axis)
+    return [1 << j for j in range(count.bit_length() - 1)]
+
+
+def halving_sum(chunks, axis, order):
+    count = lax.axis_size(axis)
+    index = lax.axis_index(axis)
+    current = chunks
+    done = []
+    for bit in order:
+        lower = 1
+        for other in axis_bits(axis):
+            if other < bit and other not in done:
+                lower *= 2
+        upper = current.shape[0] // (2 * lower)
+        split = current.reshape((upper, 2, lower) + current.shape[1:])
+        mine = (index // bit) % 2
+        keep = lax.dynamic_index_in_dim(split, mine, axis=1, keepdims=False)
+        send = lax.dynamic_index_in_dim(split, 1 - mine, axis=1, keepdims=False)
+        got = lax.ppermute(send, axis, [(k, k ^ bit) for k in range(count)])
+        current = (keep + got).reshape((upper * lower,) + current.shape[1:])
+        done.append(bit)
+    return current[0]
+
+
+def doubling_gather(piece, axis, order):
+    count = lax.axis_size(axis)
+    index = lax.axis_index(axis)
+    current = piece[None]
+    done = []
+    for bit in order:
+        lower = 1
+        for other in done:
+            if other < bit:
+                lower *= 2
+        upper = current.shape[0] // lower
+        got = lax.ppermute(current, axis, [(k, k ^ bit) for k in range(count)])
+        mine = (index // bit) % 2
+        ours = current.reshape((upper, 1, lower) + piece.shape)
+        theirs = got.reshape((upper, 1, lower) + piece.shape)
+        joined = jnp.zeros((upper, 2, lower) + piece.shape, piece.dtype)
+        joined = lax.dynamic_update_index_in_dim(joined, ours, mine, axis=1)
+        joined = lax.dynamic_update_index_in_dim(joined, theirs, 1 - mine, axis=1)
+        current = joined.reshape((upper * 2 * lower,) + piece.shape)
+        done.append(bit)
+    return current
+
+
 def reduce_gradients(gradients, rel_ids, rel_total, width):
     stacked = jnp.stack(gradients)
-    own_rows = rel_total // lax.axis_size("rel") * width
-    rel_count_piece = own_rows * lax.axis_size("rel") // width
-    rel_list = jnp.arange(rel_count_piece, dtype=jnp.int32)
+    rel_list = jnp.arange(rel_total, dtype=jnp.int32)
     weights = (rel_ids[:, None] == rel_list[None, :]).astype(jnp.float32)
     term = jnp.einsum("sk,sde->kde", weights, stacked, precision=lax.Precision.HIGHEST)
-    partial_sum = lax.psum_scatter(
-        term.reshape(rel_count_piece * width, width), "rel", scatter_dimension=0, tiled=True
-    )
-    return lax.psum(partial_sum, "bucket")
+    rel_count = lax.axis_size("rel")
+    bucket_count = lax.axis_size("bucket")
+    own = halving_sum(term.reshape(rel_count, -1, width), "rel", axis_bits("rel"))
+    part = halving_sum(own.reshape(bucket_count, -1, width), "bucket", axis_bits("bucket"))
+    return doubling_gather(part, "bucket", axis_bits("bucket")[::-1]).reshape(-1, width)
 
 
 def on_device(
@@ -110,7 +158,9 @@
     matching,
 ):
     width = relations.shape[1]
-    rel_table = lax.all_gather(relations, "rel", axis=0, tiled=True)
+    rel_table = doubling_gather(relations, "rel", axis_bits("rel")[::-1]).reshape(
+        -1, width, width
+    )
     rel_total = rel_table.shape[0]
     rel_ids = fetch_ids[0, 0]
     switch = matching[0]

time: 234 us -> 167 us (0.71)
  waiting for transfers between devices: 161 us -> 79.6 us
  starting transfers between devices: 4.01 us -> 22 us
  between operations: 14.8 us -> 1.97 us
  local copies, waits for them, and re-layouts: 19.1 us -> 28.4 us
  matrix products: 21.4 us -> 18.2 us
  other arithmetic: 13.1 us -> 15.6 us
    psum x1 -> x0, waiting for transfers between devices: 76.5 us -> none  [reduce_gradients(): return lax.psum(partial_sum, 'bucket')]
    ppermute x0 -> x10, waiting for transfers between devices: none -> 67.5 us  [the longest x5 46.2 us: halving_sum(): got = lax.ppermute(send, axis, [(k, k ^ bit) for k in range(count)])]
    reduce_scatter x1 -> x0, waiting for transfers between devices: 41.1 us -> none  [reduce_gradients(): lax.psum_scatter(term.reshape(rel_count_piece * width, width), 'rel', sca...]
    ppermute x0 -> x10, starting transfers between devices: none -> 19.9 us  [the longest x5 11.6 us: doubling_gather(): got = lax.ppermute(current, axis, [(k, k ^ bit) for k in range(count)])]
    all_gather x1 -> x0, waiting for transfers between devices: 19.7 us -> none  [on_device(): rel_table = lax.all_gather(relations, 'rel', axis=0, tiled=True)]
    ppermute x1, waiting for transfers between devices: 23.4 us -> 12.1 us  [run(): lax.ppermute(rows, 'bucket', pairs)]
    dynamic_slice x0 -> x2, local copies, waits for them, and re-layouts: none -> 8.18 us  [the longest x1 7.78 us: halving_sum(): keep = lax.dynamic_index_in_dim(split, mine, axis=1, keepdims=False)]
    reshape x0 -> x1, local copies, waits for them, and re-layouts: none -> 6.37 us  [halving_sum(): split = current.reshape((upper, 2, lower) + current.shape[1:])]
  transfers between devices with their start and end apart: 5 -> 12, of which waited for: 5 -> 12; matrix products, arithmetic and copies ran while one was open for 6% -> 7% of each run, Pallas kernels for 0% -> 0%
where the time goes in v2:
time: 167 us; the launch traced here: 166 us
  waiting for transfers between devices  79.6 us (48%)
  local copies, waits for them, and re-layouts  28.4 us (17%)
  starting transfers between devices  22 us (13%)
  matrix products  18.2 us (11%)
  other arithmetic  15.6 us (9%)
  between operations  1.97 us (1%)
    ppermute x5, waiting for transfers between devices, halving_sum(): got = lax.ppermute(send, axis, [(k, k ^ bit) for k in range(count)])  46.2 us
    ppermute x5, waiting for transfers between devices, doubling_gather(): got = lax.ppermute(current, axis, [(k, k ^ bit) for k in range(count)])  21.4 us
    ppermute x1, waiting for transfers between devices, run(): lax.ppermute(rows, 'bucket', pairs)  12.1 us
    ppermute x5, starting transfers between devices, doubling_gather(): got = lax.ppermute(current, axis, [(k, k ^ bit) for k in range(count)])  11.6 us
    ppermute x5, starting transfers between devices, halving_sum(): got = lax.ppermute(send, axis, [(k, k ^ bit) for k in range(count)])  8.27 us
    dot_general x1, matrix products, reduce_gradients(): jnp.einsum('sk,sde->kde', weights, stacked, precision=lax.Precision.HIGHEST)  8.23 us
    dynamic_slice x1, local copies, waits for them, and re-layouts, halving_sum(): keep = lax.dynamic_index_in_dim(split, mine, axis=1, keepdims=False)  7.78 us
    reshape x1, local copies, waits for them, and re-layouts, halving_sum(): split = current.reshape((upper, 2, lower) + current.shape[1:])  6.37 us
  transfers between devices with their start and end apart: 12, of which 12 were waited for; matrix products, arithmetic and copies ran while one was open for 7% of the time, Pallas kernels for 0%

profile of v2, /device:TPU:0, one launch (start us, length us, event | category | flops | bytes accessed | tf_op | source)
XLA Modules:
  0.0 165.8 jit_solution(8112200118427982987)
XLA Ops:
  0.6 3.1 %collective-permute-start.14 = (bf16[1,1,512,512]{3,2,1,0:T(8,128)(2,1)}, bf16[1,1,512,512]{3,2,1,0:T(8,128)(2,1)S(1)}, u32[]{:S(2)}, u32[]{:S(2)}) collective-permute-start(bf16[1,1,512,512]{3,2,1,0:T(8,128)(2,1)} %bitcast.150), channel_id=1, source_target_pairs={{0,2},{1,3},{2,0},{3,1},{4,6},{5,7},{6,4},{7,5},{8,10},{9,11},{10,... | collective-permute-start | bytes 1572872 | tf_op jit(solution)/shard_map/ppermute | solution.py:123
  4.4 1.1 convert_element_type.105
  5.5 1.8 %convert_element_type.103 = bf16[256,512]{1,0:T(8,128)(2,1)} convert(f32[256,512]{1,0:T(8,128)} %param.20) | non-fusion elementwise | flops 131072 | bytes 786432 | tf_op jit(solution)/shard_map/convert_element_type | solution.py:43
  7.3 0.8 compare_and_fusion
  8.2 7.6 %collective-permute-done.14 = bf16[1,1,512,512]{3,2,1,0:T(8,128)(2,1)S(1)} collective-permute-done((bf16[1,1,512,512]{3,2,1,0:T(8,128)(2,1)}, bf16[1,1,512,512]{3,2,1,0:T(8,128)(2,1)S(1)}, u32[]{:S(2)}, u32[]{:S(2)}) %collective-permute-start.14) | collective-permute-done | bytes 524320 | tf_op jit(solution)/shard_map/ppermute | solution.py:123
  16.0 0.6 fusion.59
  16.6 0.6 compare_select_fusion
  17.5 1.1 collective-permute-done.15
  18.7 0.6 gather_fusion.1
  19.3 1.6 gather_fusion
  20.9 1.5 broadcast_select_fusion
  23.5 0.5 fusion.16
  24.8 0.5 fusion.17
  26.5 1.0 convolution_convert_fusion.1
  29.2 15.6 %conditional.4 = (f32[256,512]{1,0:T(8,128)}, f32[256]{0:T(256)}, f32[256,512]{1,0:T(8,128)S(1)}) conditional(s32[]{:T(128)} %bitcast.17, (f32[256,512]{1,0:T(8,128)S(1)}, f32[256,512]{1,0:T(8,128)S(1)}, f32[256]{0:T(256)S(1)}, f32[256,512]{1,0:T(8,128)S(1)}, f32[256,512]{1,0:T(8,128)S(1)}, ...), branch_computations={%region_2.4_spmd, %region_3.5_spmd, %region_4.6_spmd, %region_5.7_... | conditional | flops 655616 | bytes 5778540
  29.5 1.8 %collective-permute-start = (f32[256,512]{1,0:T(8,128)S(1)}, f32[256,512]{1,0:T(8,128)}, u32[]{:S(2)}, u32[]{:S(2)}) collective-permute-start(f32[256,512]{1,0:T(8,128)S(1)} %divide_subtract_fusion), channel_id=1, source_target_pairs={{0,4},{4,0},{8,12},{12,8},{16,20},{20,16},{24,28},{28,24},{1,5},{5... | collective-permute-start | bytes 1572872 | tf_op jit(solution)/shard_map/cond/branch_0_fun/ppermute | solution.py:78
  31.6 12.1 %collective-permute-done = f32[256,512]{1,0:T(8,128)} collective-permute-done((f32[256,512]{1,0:T(8,128)S(1)}, f32[256,512]{1,0:T(8,128)}, u32[]{:S(2)}, u32[]{:S(2)}) %collective-permute-start) | collective-permute-done | bytes 524320 | tf_op jit(solution)/shard_map/cond/branch_0_fun/ppermute | solution.py:78
  43.7 1.0 copy.82
  46.5 0.5 fusion.19
  47.3 0.7 copy-done.4
  48.7 2.5 %pad_maximum_fusion = f32[4,512,512]{1,2,0:T(8,128)} fusion(f32[1,512,512]{1,2,0:T(8,128)S(1)} %convolution_bitcast_fusion, f32[1,512,512]{1,2,0:T(8,128)S(1)} %convolution_bitcast_fusion.1, f32[1,512,512]{1,2,0:T(8,128)S(1)} %convolution_bitcast_fusion.2, f32[1,512,512]{1,2,0:T(8,128)S(1)} %convolution_bitcast_fusion.3), kind=kLoop, calls=%fused_computation.23 | loop fusion | flops 3145728 | bytes 8388608 | tf_op jit(solution)/shard_map/stack | solution.py:136
  51.2 5.5 %copy.35 = f32[4,512,512]{2,0,1:T(4,128)} copy(f32[4,512,512]{1,2,0:T(8,128)} %pad_maximum_fusion) | data formatting | bytes 8388608 | tf_op jit(solution)/shard_map/stack | solution.py:136
  56.6 8.2 %fusion.40 = f32[4,512,512]{2,0,1:T(4,128)} fusion(f32[4,512,512]{2,0,1:T(4,128)} %copy.35, s32[4]{0:T(128)S(1)} %bitcast.151), kind=kOutput, calls=%fused_computation.139 | convolution fusion | flops 50331664 | bytes 8388624 | tf_op jit(solution)/shard_map/sk,sde->kde/dot_general | solution.py:139
  64.9 6.4 %reshape.127 = f32[2,2,1,512,512]{4,1,0,3,2:T(2,128)} reshape(f32[4,512,512]{2,0,1:T(4,128)} %fusion.40) | data formatting | bytes 8388608 | tf_op jit(solution)/shard_map/reshape | solution.py:102
  71.2 7.8 %constant_dynamic-slice_fusion.3 = (f32[2,1,1,512,512]{4,1,0,3,2:T(1,128)S(1)}, f32[2,1,1,512,512]{4,1,0,3,2:T(1,128)S(1)}) fusion(f32[2,2,1,512,512]{4,1,0,3,2:T(2,128)} %reshape.127, s32[]{:T(128)S(6)} %select_n.166, s32[]{:T(128)S(6)} %select_n.167), kind=kLoop, calls=%fused_computation.132 | loop fusion | bytes 8388616 | tf_op jit(solution)/shard_map/jit(dynamic_index_in_dim)/dynamic_slice | solution.py:104
  79.5 4.1 %collective-permute-done.16 = f32[2,1,512,512]{3,2,1,0:T(8,128)S(1)} collective-permute-done((f32[2,1,512,512]{3,2,1,0:T(8,128)S(1)}, f32[2,1,512,512]{3,2,1,0:T(8,128)S(1)}, u32[]{:S(2)}, u32[]{:S(2)}) %collective-permute-start.16) | collective-permute-done | bytes 2097184 | tf_op jit(solution)/shard_map/ppermute | solution.py:106
  83.7 0.5 bitcast_add_fusion
  84.2 1.1 constant_dynamic-slice_fusion.1
  85.3 1.7 %collective-permute-start.17 = (f32[1,1,512,512]{3,2,1,0:T(8,128)}, f32[1,1,512,512]{3,2,1,0:T(8,128)}, u32[]{:S(2)}, u32[]{:S(2)}) collective-permute-start(f32[1,1,512,512]{3,2,1,0:T(8,128)} %constant_dynamic-slice_fusion.1), channel_id=1, source_target_pairs={{0,2},{1,3},{2,0},{3,1},{4,6},{5,7},{6,4},{7,5},{8,10},{9,11},{10,... | collective-permute-start | bytes 3145736 | tf_op jit(solution)/shard_map/ppermute | solution.py:106
  87.0 23.8 %collective-permute-done.17 = f32[1,1,512,512]{3,2,1,0:T(8,128)} collective-permute-done((f32[1,1,512,512]{3,2,1,0:T(8,128)}, f32[1,1,512,512]{3,2,1,0:T(8,128)}, u32[]{:S(2)}, u32[]{:S(2)}) %collective-permute-start.17) | collective-permute-done | bytes 1048608 | tf_op jit(solution)/shard_map/ppermute | solution.py:106
  110.8 1.4 dynamic-slice_add_fusion
  112.3 1.8 %collective-permute-start.18 = (f32[4,1,64,512]{3,2,0,1:T(8,128)S(1)}, f32[4,1,64,512]{3,2,0,1:T(8,128)S(1)}, u32[]{:S(2)}, u32[]{:S(2)}) collective-permute-start(f32[4,1,64,512]{3,2,0,1:T(8,128)S(1)} %dynamic-slice_bitcast_fusion), channel_id=1, source_target_pairs={{0,4},{4,0},{8,12},{12,8},{16,20},{20,16},{24,28},{28,24},{1,5},{5... | collective-permute-start | bytes 1572872 | tf_op jit(solution)/shard_map/ppermute | solution.py:106
  114.8 10.6 %collective-permute-done.18 = f32[4,1,64,512]{3,2,0,1:T(8,128)S(1)} collective-permute-done((f32[4,1,64,512]{3,2,0,1:T(8,128)S(1)}, f32[4,1,64,512]{3,2,0,1:T(8,128)S(1)}, u32[]{:S(2)}, u32[]{:S(2)}) %collective-permute-start.18) | collective-permute-done | bytes 524320 | tf_op jit(solution)/shard_map/ppermute | solution.py:106
  125.6 1.9 %collective-permute-start.19 = (f32[2,1,64,512]{3,2,0,1:T(8,128)S(1)}, f32[2,1,64,512]{3,2,0,1:T(8,128)S(1)}, u32[]{:S(2)}, u32[]{:S(2)}) collective-permute-start(f32[2,1,64,512]{3,2,0,1:T(8,128)S(1)} %dynamic-slice_bitcast_fusion.1), channel_id=1, source_target_pairs={{0,8},{4,12},{8,0},{12,4},{16,24},{20,28},{24,16},{28,20},{1,9},{5... | collective-permute-start | bytes 786440 | tf_op jit(solution)/shard_map/ppermute | solution.py:106
  128.1 4.3 %collective-permute-done.19 = f32[2,1,64,512]{3,2,0,1:T(8,128)S(1)} collective-permute-done((f32[2,1,64,512]{3,2,0,1:T(8,128)S(1)}, f32[2,1,64,512]{3,2,0,1:T(8,128)S(1)}, u32[]{:S(2)}, u32[]{:S(2)}) %collective-permute-start.19) | collective-permute-done | bytes 262176 | tf_op jit(solution)/shard_map/ppermute | solution.py:106
  132.4 2.8 %collective-permute-start.20 = (f32[1,1,64,512]{3,2,0,1:T(8,128)S(1)}, f32[1,1,64,512]{3,2,0,1:T(8,128)S(1)}, u32[]{:S(2)}, u32[]{:S(2)}) collective-permute-start(f32[1,1,64,512]{3,2,0,1:T(8,128)S(1)} %constant_dynamic-slice_fusion), channel_id=1, source_target_pairs={{0,16},{4,20},{8,24},{12,28},{16,0},{20,4},{24,8},{28,12},{1,17},{... | collective-permute-start | bytes 393224 | tf_op jit(solution)/shard_map/ppermute | solution.py:106
  135.2 1.2 fusion.56
  136.4 3.3 %collective-permute-done.20 = f32[1,1,64,512]{3,2,0,1:T(8,128)S(1)} collective-permute-done((f32[1,1,64,512]{3,2,0,1:T(8,128)S(1)}, f32[1,1,64,512]{3,2,0,1:T(8,128)S(1)}, u32[]{:S(2)}, u32[]{:S(2)}) %collective-permute-start.20) | collective-permute-done | bytes 131104 | tf_op jit(solution)/shard_map/ppermute | solution.py:106
  139.8 1.5 collective-permute-start.21
  141.3 4.4 %collective-permute-done.21 = f32[1,64,512]{2,1,0:T(8,128)S(1)} collective-permute-done((f32[1,64,512]{2,1,0:T(8,128)S(1)}, f32[1,64,512]{2,1,0:T(8,128)S(1)}, u32[]{:S(2)}, u32[]{:S(2)}) %collective-permute-start.21) | collective-permute-done | bytes 131104 | tf_op jit(solution)/shard_map/ppermute | solution.py:123
  145.8 5.4 %collective-permute-start.22 = (f32[2,64,512]{2,1,0:T(8,128)S(1)}, f32[2,64,512]{2,1,0:T(8,128)S(1)}, u32[]{:S(2)}, u32[]{:S(2)}) collective-permute-start(f32[2,64,512]{2,1,0:T(8,128)S(1)} %bitcast.148), channel_id=1, source_target_pairs={{0,8},{4,12},{8,0},{12,4},{16,24},{20,28},{24,16},{28,20},{1,9},{5... | collective-permute-start | bytes 786440 | tf_op jit(solution)/shard_map/ppermute | solution.py:123
  151.2 2.0 %divide_subtract_fusion.7 = f32[256,512]{1,0:T(8,128)} fusion(f32[256,512]{1,0:T(8,128)} %get-tuple-element.146, f32[256,512]{1,0:T(8,128)S(1)} %get-tuple-element.255, f32[256]{0:T(256)S(1)} %get-tuple-element.230), kind=kLoop, calls=%fused_computation.84 | loop fusion | flops 393216 | bytes 1573888 | tf_op jit(solution)/shard_map/sub | solution.py:28
  153.2 2.3 %collective-permute-done.22 = f32[2,64,512]{2,1,0:T(8,128)S(1)} collective-permute-done((f32[2,64,512]{2,1,0:T(8,128)S(1)}, f32[2,64,512]{2,1,0:T(8,128)S(1)}, u32[]{:S(2)}, u32[]{:S(2)}) %collective-permute-start.22) | collective-permute-done | bytes 262176 | tf_op jit(solution)/shard_map/ppermute | solution.py:123
  155.6 1.6 collective-permute-start.23
  157.1 0.6 fusion.57
  157.7 1.0 divide_subtract_fusion.8
  158.9 5.9 %collective-permute-done.23 = f32[4,64,512]{2,1,0:T(8,128)S(1)} collective-permute-done((f32[4,64,512]{2,1,0:T(8,128)S(1)}, f32[4,64,512]{2,1,0:T(8,128)S(1)}, u32[]{:S(2)}, u32[]{:S(2)}) %collective-permute-start.23) | collective-permute-done | bytes 524320 | tf_op jit(solution)/shard_map/ppermute | solution.py:123
  164.9 1.0 copy-done.9
  (113 shorter events, 10.9 us)
Async XLA Ops:
  0.6 7.5 %copy-start.12 = (bf16[1,512,512]{2,1,0:T(8,128)(2,1)S(1)}, bf16[1,512,512]{2,1,0:T(8,128)(2,1)}, u32[]{:S(2)}) copy-start(bf16[1,512,512]{2,1,0:T(8,128)(2,1)} %param.24) | copy-start | bytes 1572868
  0.6 15.2 %collective-permute-start.14 = (bf16[1,1,512,512]{3,2,1,0:T(8,128)(2,1)}, bf16[1,1,512,512]{3,2,1,0:T(8,128)(2,1)S(1)}, u32[]{:S(2)}, u32[]{:S(2)}) collective-permute-start(bf16[1,1,512,512]{3,2,1,0:T(8,128)(2,1)} %bitcast.150), channel_id=1, source_target_pairs={{0,2},{1,3},{2,0},{3,1},{4,6},{5,7},{6,4},{7,5},{8,10},{9,11},{10,... | collective-permute-start | bytes 1572872 | tf_op jit(solution)/shard_map/ppermute | solution.py:123
  5.4 10.5 %copy-start.20 = (s32[1,1,2,512]{3,2,1,0:T(2,128)S(1)}, s32[1,1,2,512]{3,2,1,0:T(2,128)}, u32[]{:S(2)}) copy-start(s32[1,1,2,512]{3,2,1,0:T(2,128)} %param.26) | copy-start | bytes 12292
  5.4 10.6 %copy-start.21 = (s32[1,1,2,512]{3,2,1,0:T(2,128)S(1)}, s32[1,1,2,512]{3,2,1,0:T(2,128)}, u32[]{:S(2)}) copy-start(s32[1,1,2,512]{3,2,1,0:T(2,128)} %param.27) | copy-start | bytes 12292
  5.5 11.1 %copy-start.22 = (s32[1,1,2,512]{3,2,1,0:T(2,128)S(1)}, s32[1,1,2,512]{3,2,1,0:T(2,128)}, u32[]{:S(2)}) copy-start(s32[1,1,2,512]{3,2,1,0:T(2,128)} %param.29) | copy-start | bytes 12292
  5.5 11.1 %copy-start.23 = (s32[1,1,2,512]{3,2,1,0:T(2,128)S(1)}, s32[1,1,2,512]{3,2,1,0:T(2,128)}, u32[]{:S(2)}) copy-start(s32[1,1,2,512]{3,2,1,0:T(2,128)} %param.28) | copy-start | bytes 12292
  15.9 2.7 %collective-permute-start.15 = (bf16[2,1,512,512]{3,2,0,1:T(8,128)(2,1)S(1)}, bf16[2,1,512,512]{3,2,0,1:T(8,128)(2,1)S(1)}, u32[]{:S(2)}, u32[]{:S(2)}) collective-permute-start(bf16[2,1,512,512]{3,2,0,1:T(8,128)(2,1)S(1)} %bitcast.140), channel_id=1, source_target_pairs={{0,1},{1,0},{2,3},{3,2},{4,5},{5,4},{6,7},{7,6},{8,9},{9,8},{10,11... | collective-permute-start | bytes 3145736 | tf_op jit(solution)/shard_map/ppermute | solution.py:123
  20.9 1.5 copy-start.6
  22.4 5.1 %copy-start.2 = (bf16[2,512,512]{2,1,0:T(8,128)(2,1)}, bf16[2,512,512]{2,1,0:T(8,128)(2,1)S(1)}, u32[]{:S(2)}) copy-start(bf16[2,512,512]{2,1,0:T(8,128)(2,1)S(1)} %get-tuple-element.256) | copy-start | bytes 3145732
  25.3 1.0 copy-start.19
  25.3 1.0 copy-start.1
  26.5 1.3 copy-start.7
  27.8 17.0 %copy-start.15 = (bf16[256,512]{1,0:T(8,128)(2,1)}, bf16[256,512]{1,0:T(8,128)(2,1)S(1)}, u32[]{:S(2)}) copy-start(bf16[256,512]{1,0:T(8,128)(2,1)S(1)} %convolution_convert_fusion.3) | copy-start | bytes 786436
  28.2 1.0 copy-start
  28.2 1.0 copy-start.17
  29.5 14.1 %collective-permute-start = (f32[256,512]{1,0:T(8,128)S(1)}, f32[256,512]{1,0:T(8,128)}, u32[]{:S(2)}, u32[]{:S(2)}) collective-permute-start(f32[256,512]{1,0:T(8,128)S(1)} %divide_subtract_fusion), channel_id=1, source_target_pairs={{0,4},{4,0},{8,12},{12,8},{16,20},{20,16},{24,28},{28,24},{1,5},{5... | collective-permute-start | bytes 1572872 | tf_op jit(solution)/shard_map/cond/branch_0_fun/ppermute | solution.py:78
  31.3 12.4 %collective-permute-start.1 = (f32[256]{0:T(256)S(1)}, f32[256]{0:T(256)}, u32[]{:S(2)}, u32[]{:S(2)}) collective-permute-start(f32[256]{0:T(256)S(1)} %get-tuple-element.217), channel_id=1, source_target_pairs={{0,4},{4,0},{8,12},{12,8},{16,20},{20,16},{24,28},{28,24},{1,5},{5... | collective-permute-start | bytes 3080 | tf_op jit(solution)/shard_map/cond/branch_0_fun/ppermute | solution.py:78
  44.8 0.7 copy-start.24
  44.8 0.7 copy-start.26
  44.8 1.4 copy-start.13
  44.8 1.7 %copy-start.25 = (f32[1,1,1,512]{3,2,1,0:T(1,128)S(1)}, f32[1,1,1,512]{3,2,1,0:T(1,128)}, u32[]{:S(2)}) copy-start(f32[1,1,1,512]{3,2,1,0:T(1,128)} %get-tuple-element.240) | copy-start | bytes 6148
  46.0 2.0 %copy-start.8 = (bf16[256,512]{1,0:T(8,128)(2,1)S(1)}, bf16[256,512]{1,0:T(8,128)(2,1)}, u32[]{:S(2)}) copy-start(bf16[256,512]{1,0:T(8,128)(2,1)} %copy-done.7) | copy-start | bytes 786436
  47.0 1.3 copy-start.10
  47.3 0.7 copy-start.4
  51.2 5.5 %copy-start.18 = (s32[1,1,4]{2,1,0:T(1,128)S(1)}, s32[1,1,4]{2,1,0:T(1,128)}, u32[]{:S(2)}) copy-start(s32[1,1,4]{2,1,0:T(1,128)} %param.25) | copy-start | bytes 52
  79.4 4.2 %collective-permute-start.16 = (f32[2,1,512,512]{3,2,1,0:T(8,128)S(1)}, f32[2,1,512,512]{3,2,1,0:T(8,128)S(1)}, u32[]{:S(2)}, u32[]{:S(2)}) collective-permute-start(f32[2,1,512,512]{3,2,1,0:T(8,128)S(1)} %bitcast.143), channel_id=1, source_target_pairs={{0,1},{1,0},{2,3},{3,2},{4,5},{5,4},{6,7},{7,6},{8,9},{9,8},{10,11... | collective-permute-start | bytes 6291464 | tf_op jit(solution)/shard_map/ppermute | solution.py:106
  85.3 25.5 %collective-permute-start.17 = (f32[1,1,512,512]{3,2,1,0:T(8,128)}, f32[1,1,512,512]{3,2,1,0:T(8,128)}, u32[]{:S(2)}, u32[]{:S(2)}) collective-permute-start(f32[1,1,512,512]{3,2,1,0:T(8,128)} %constant_dynamic-slice_fusion.1), channel_id=1, source_target_pairs={{0,2},{1,3},{2,0},{3,1},{4,6},{5,7},{6,4},{7,5},{8,10},{9,11},{10,... | collective-permute-start | bytes 3145736 | tf_op jit(solution)/shard_map/ppermute | solution.py:106
  87.0 27.0 %copy-start.3 = (bf16[2,512,512]{2,1,0:T(8,128)(2,1)S(1)}, bf16[2,512,512]{2,1,0:T(8,128)(2,1)}, u32[]{:S(2)}) copy-start(bf16[2,512,512]{2,1,0:T(8,128)(2,1)} %copy-done.2) | copy-start | bytes 3145732
  87.0 27.4 %copy-start.5 = (bf16[256,512]{1,0:T(8,128)(2,1)S(1)}, bf16[256,512]{1,0:T(8,128)(2,1)}, u32[]{:S(2)}) copy-start(bf16[256,512]{1,0:T(8,128)(2,1)} %copy-done.4) | copy-start | bytes 786436
  112.3 13.2 %collective-permute-start.18 = (f32[4,1,64,512]{3,2,0,1:T(8,128)S(1)}, f32[4,1,64,512]{3,2,0,1:T(8,128)S(1)}, u32[]{:S(2)}, u32[]{:S(2)}) collective-permute-start(f32[4,1,64,512]{3,2,0,1:T(8,128)S(1)} %dynamic-slice_bitcast_fusion), channel_id=1, source_target_pairs={{0,4},{4,0},{8,12},{12,8},{16,20},{20,16},{24,28},{28,24},{1,5},{5... | collective-permute-start | bytes 1572872 | tf_op jit(solution)/shard_map/ppermute | solution.py:106
  114.4 13.1 %copy-start.16 = (bf16[256,512]{1,0:T(8,128)(2,1)S(1)}, bf16[256,512]{1,0:T(8,128)(2,1)}, u32[]{:S(2)}) copy-start(bf16[256,512]{1,0:T(8,128)(2,1)} %copy-done.15) | copy-start | bytes 786436
  114.4 13.3 %copy-start.11 = (bf16[256,256]{1,0:T(8,128)(2,1)S(1)}, bf16[256,256]{1,0:T(8,128)(2,1)}, u32[]{:S(2)}) copy-start(bf16[256,256]{1,0:T(8,128)(2,1)} %copy-done.10) | copy-start | bytes 393220
  114.4 13.3 %copy-start.14 = (bf16[256,512]{1,0:T(8,128)(2,1)S(1)}, bf16[256,512]{1,0:T(8,128)(2,1)}, u32[]{:S(2)}) copy-start(bf16[256,512]{1,0:T(8,128)(2,1)} %convolution_convert_fusion.1) | copy-start | bytes 786436
  125.6 6.8 %collective-permute-start.19 = (f32[2,1,64,512]{3,2,0,1:T(8,128)S(1)}, f32[2,1,64,512]{3,2,0,1:T(8,128)S(1)}, u32[]{:S(2)}, u32[]{:S(2)}) collective-permute-start(f32[2,1,64,512]{3,2,0,1:T(8,128)S(1)} %dynamic-slice_bitcast_fusion.1), channel_id=1, source_target_pairs={{0,8},{4,12},{8,0},{12,4},{16,24},{20,28},{24,16},{28,20},{1,9},{5... | collective-permute-start | bytes 786440 | tf_op jit(solution)/shard_map/ppermute | solution.py:106
  132.4 7.3 %collective-permute-start.20 = (f32[1,1,64,512]{3,2,0,1:T(8,128)S(1)}, f32[1,1,64,512]{3,2,0,1:T(8,128)S(1)}, u32[]{:S(2)}, u32[]{:S(2)}) collective-permute-start(f32[1,1,64,512]{3,2,0,1:T(8,128)S(1)} %constant_dynamic-slice_fusion), channel_id=1, source_target_pairs={{0,16},{4,20},{8,24},{12,28},{16,0},{20,4},{24,8},{28,12},{1,17},{... | collective-permute-start | bytes 393224 | tf_op jit(solution)/shard_map/ppermute | solution.py:106
  139.8 6.0 %collective-permute-start.21 = (f32[1,64,512]{2,1,0:T(8,128)S(1)}, f32[1,64,512]{2,1,0:T(8,128)S(1)}, u32[]{:S(2)}, u32[]{:S(2)}) collective-permute-start(f32[1,64,512]{2,1,0:T(8,128)S(1)} %fusion.38), channel_id=1, source_target_pairs={{0,16},{4,20},{8,24},{12,28},{16,0},{20,4},{24,8},{28,12},{1,17},{... | collective-permute-start | bytes 393224 | tf_op jit(solution)/shard_map/ppermute | solution.py:123
  145.8 9.8 %collective-permute-start.22 = (f32[2,64,512]{2,1,0:T(8,128)S(1)}, f32[2,64,512]{2,1,0:T(8,128)S(1)}, u32[]{:S(2)}, u32[]{:S(2)}) collective-permute-start(f32[2,64,512]{2,1,0:T(8,128)S(1)} %bitcast.148), channel_id=1, source_target_pairs={{0,8},{4,12},{8,0},{12,4},{16,24},{20,28},{24,16},{28,20},{1,9},{5... | collective-permute-start | bytes 786440 | tf_op jit(solution)/shard_map/ppermute | solution.py:123
  155.6 9.2 %collective-permute-start.23 = (f32[4,64,512]{2,1,0:T(8,128)S(1)}, f32[4,64,512]{2,1,0:T(8,128)S(1)}, u32[]{:S(2)}, u32[]{:S(2)}) collective-permute-start(f32[4,64,512]{2,1,0:T(8,128)S(1)} %bitcast.146), channel_id=1, source_target_pairs={{0,4},{4,0},{8,12},{12,8},{16,20},{20,16},{24,28},{28,24},{1,5},{5... | collective-permute-start | bytes 1572872 | tf_op jit(solution)/shard_map/ppermute | solution.py:123
  164.9 1.0 copy-start.9
